TPU v7x, 256 devices: a whole 4x4x8 slice. The times are simulated.
256 devices in a mesh: circ: 8 (over y_lo, x), span: 32 (over y_hi, z, core).
Axes of the slice: x: 4, y: 4 (y_hi: 2, y_lo: 2; y = y_hi * 2 + y_lo), z: 8, core: 2. Of those that a mesh axis runs over, the one named last changes fastest.
Arguments:
- q_old: float32 [5, 32, 4096, 128], P(None, 'circ', 'span'), may hold values from -6 to 6
- pseudo_rate: float32 [32, 4096, 128], P('circ', 'span'), may hold values from 0.15 to 0.45
- flux_jacobians: float32 [3, 5, 5], replicated, may hold values from -2.5 to 2.5
- rotor_face: float32 [5, 32, 4096], P(None, 'circ', 'span'), may hold values from -6 to 6
- offsets: int32 [4096], P('span'), may hold values from 0 to 31
- owners: int32 [8, 128, 4], P('circ', 'span'), may hold values from 0 to 31, all different within a row; in each aligned block of 4 rows (0 to 3, 4 to 7, ..., all dimensions but the last counted through in order) at most 2 rows name the same one
- slots: int32 [8, 128, 4], P('circ', 'span'), may hold values from 0 to 3
- weight_idx: int32 [8, 128, 4], P('circ', 'span'), may hold values from 0 to 15
- weight_table: float32 [16], replicated, may hold values from 0.3 to 1
Outputs:
- q_new: float32 [5, 32, 4096, 128], P(None, 'circ', 'span')
Inputs may be any that keep to these rules, and one draw needn't show every extreme that they name: The 4 owners of one rotor panel differ; among the 4 rotor panels of one device in one circumferential block, no owner is named more than 2 times, and that count is reached.
All inputs are finite; a program needn't handle non-finite values.
Results may differ from a plain program's by a relative error of at most 0.000068.
Values sent between devices are 32-bit elements; how exact they have to be, the bound alone decides.
No kernel may reach another device: no remote copies, remote signals or barrier semaphores. Data moves between devices by JAX's collectives and lax.ppermute only.
A program may use at most 64 MiB of HBM per device.

v0:
```python
import jax
import jax.numpy as jnp
from jax import lax
from jax.sharding import PartitionSpec as P

NF = 5
KP_DEV = 4
PW = 32
inv_step = 0.5
viscosity = 0.1


def with_halo(block, sides, width):
    for axis, dim in sides:
        count = lax.axis_size(axis)
        forward = [(i, i + 1) for i in range(count - 1)]
        forward.append((count - 1, 0))
        backward = [(target, source) for source, target in forward]
        low = lax.ppermute(
            lax.slice_in_dim(block, block.shape[dim] - width, None, axis=dim), axis, forward
        )
        high = lax.ppermute(lax.slice_in_dim(block, 0, width, axis=dim), axis, backward)
        block = jnp.concatenate([low, block, high], axis=dim)
    return block


def contract(matrix, values):
    return jnp.einsum("fg,gtsa->ftsa", matrix, values, precision=lax.Precision.HIGHEST)


def advance(padded, current, previous, rate_cells, inlet_plane, jacobians):
    circ_up = padded[:, 2:, 1:-1]
    circ_down = padded[:, :-2, 1:-1]
    span_up = padded[:, 1:-1, 2:]
    span_down = padded[:, 1:-1, :-2]
    zero_column = jnp.zeros_like(current[..., :1])
    axial_up = jnp.concatenate([current[..., 1:], zero_column], axis=-1)
    axial_down = jnp.concatenate([inlet_plane[..., None], current[..., :-1]], axis=-1)
    convection = contract(jacobians[0], circ_up - circ_down)
    convection = convection + contract(jacobians[1], span_up - span_down)
    convection = convection + contract(jacobians[2], axial_up - axial_down)
    laplacian = (
        circ_up + circ_down + (span_up + span_down) + (axial_up + axial_down) - 6.0 * current
    )
    residual = inv_step * (current - previous) + 0.5 * convection - viscosity * laplacian
    return current - rate_cells[None] * residual


def wall_zero(field_array, width):
    span_index = lax.axis_index("span")
    span_count = lax.axis_size("span")
    length = field_array.shape[2]
    position = jnp.arange(length, dtype=jnp.int32)
    at_hub = jnp.logical_and(span_index == 0, position < width)
    at_tip = jnp.logical_and(span_index == span_count - 1, position >= length - width)
    keeping = jnp.logical_not(jnp.logical_or(at_hub, at_tip)).astype(field_array.dtype)
    keeping = keeping.reshape(1, 1, length, 1)
    return field_array * keeping


def body(
    q_old, pseudo_rate, flux_jacobians, rotor_face, offsets, owners, slots, weight_idx, weight_table
):
    circ_count = lax.axis_size("circ")
    rows_local = rotor_face.shape[1]
    total_rows = rows_local * circ_count
    row_iota = jnp.arange(rows_local, dtype=jnp.int32)
    all_rows = lax.all_gather(rotor_face, "circ", axis=1, tiled=True)
    first_row = lax.axis_index("circ") * rows_local
    source_rows = (first_row + row_iota[:, None] - offsets[None, :]) % total_rows
    rotated = jnp.take_along_axis(all_rows, source_rows[None], axis=1)
    panels = rotated.reshape(NF, rows_local, KP_DEV, PW)
    table_ids = jnp.arange(weight_table.shape[0], dtype=jnp.int32)
    weights = jnp.sum(jnp.where(weight_idx[..., None] == table_ids, weight_table, 0.0), axis=-1)
    targets = owners[0] * KP_DEV + slots[0]
    local_weights = weights[0]
    panel_ids = jnp.arange(KP_DEV * lax.axis_size("span"), dtype=jnp.int32)
    mixing = jnp.sum(
        jnp.where(targets[None] == panel_ids[:, None, None], local_weights[None], 0.0), axis=-1
    )
    span_count = lax.axis_size("span")
    contributions = jnp.einsum("gk,ftkp->gftp", mixing, panels, precision=lax.Precision.HIGHEST)
    contributions = contributions.reshape((span_count, KP_DEV) + contributions.shape[1:])
    received = lax.all_to_all(contributions, "span", 0, 0, tiled=True)
    own_panels = jnp.sum(received, axis=0)
    inlet_plane = jnp.transpose(own_panels, (1, 2, 0, 3)).reshape(NF, rows_local, KP_DEV * PW)

    def sweep(current):
        padded = with_halo(current, (("circ", 1), ("span", 2)), 1)
        padded = wall_zero(padded, 1)
        return advance(padded, current, q_old, pseudo_rate, inlet_plane, flux_jacobians)

    first_pass = sweep(q_old)
    return sweep(first_pass)


def solution(mesh):
    return jax.shard_map(
        body,
        mesh=mesh,
        in_specs=(
            P(None, "circ", "span", None),
            P("circ", "span", None),
            P(),
            P(None, "circ", "span"),
            P("span"),
            P("circ", "span", None),
            P("circ", "span", None),
            P("circ", "span", None),
            P(),
        ),
        out_specs=P(None, "circ", "span", None),
        check_vma=False,
    )
```

profile of v0, /device:TPU:6, one launch (start us, length us, event | category | flops | bytes accessed | tf_op | source)
XLA Modules:
  0.0 128.1 jit_solution(10286612032993077256)
XLA Ops:
  0.0 1.2 fusion.49
  1.2 1.0 copy.118
  2.2 1.5 %collective-permute-start = (f32[5,1,128,128]{3,0,2,1:T(8,128)}, f32[5,1,128,128]{3,0,2,1:T(8,128)}, u32[]{:S(2)}, u32[]{:S(2)}) collective-permute-start(f32[5,1,128,128]{3,0,2,1:T(8,128)} %copy.118), channel_id=1, source_target_pairs={{0,32},{32,64},{64,96},{96,128},{128,160},{160,192},{192,224},{224... | collective-permute-start | bytes 983048 | tf_op jit(solution)/shard_map/ppermute | solution.py:19
  3.7 1.0 copy.119
  6.0 36.6 %all_gather.3 = f32[5,32,128]{2,0,1:T(8,128)S(1)} all-gather(f32[5,4,128]{2,0,1:T(8,128)S(1)} %copy.76), channel_id=1, replica_groups=mesh['circ'=8,'span'=32] {'circ'}, dimensions={1}, use_global_device_ids=true | all-gather | bytes 92160 | tf_op jit(solution)/shard_map/all_gather | solution.py:68
  43.2 3.5 %gather_fusion = f32[512,5]{1,0:T(8,128)S(1)} fusion(f32[5,32,128]{0,2,1:T(8,128)S(1)} %copy.77, s32[512]{0:T(512)S(1)} %fusion.41), kind=kCustom, calls=%fused_computation | custom fusion | bytes 24576 | tf_op jit(solution)/shard_map/jit(take_along_axis)/gather | solution.py:71
  47.0 1.3 fusion.34
  48.3 0.8 copy.80
  49.2 1.6 %reshape.183 = f32[32,1,2560]{2,1,0:T(1,128)} reshape(f32[32,4,5,4,32]{4,3,2,1,0:T(4,128)S(1)} %copy.80) | data formatting | bytes 655360
  50.7 11.2 %all-to-all-start = ((f32[32,1,2560]{2,1,0:T(1,128)}), f32[32,1,2560]{2,1,0:T(1,128)S(1)}, u32[]{:S(2)}, u32[]{:S(2)}) async-start(f32[32,1,2560]{2,1,0:T(1,128)} %reshape.183), calls=%async_computation | async-start | bytes 655360 | tf_op jit(solution)/shard_map/all_to_all | solution.py:84
  62.4 1.1 constant_dynamic-update-slice_fusion.1
  63.5 0.8 copy_dynamic-update-slice_fusion
  64.4 1.1 constant_dynamic-update-slice_fusion
  65.8 5.2 %collective-permute-start.3 = (f32[5,6,1,128]{3,0,2,1:T(8,128)S(1)}, f32[5,6,1,128]{3,0,2,1:T(8,128)S(1)}, u32[]{:S(2)}, u32[]{:S(2)}) collective-permute-start(f32[5,6,1,128]{3,0,2,1:T(8,128)S(1)} %get-tuple-element.8), channel_id=1, source_target_pairs={{1,0},{2,1},{3,2},{4,3},{5,4},{6,5},{7,6},{8,7},{9,8},{10,9},{11,1... | collective-permute-start | bytes 46088 | tf_op jit(solution)/shard_map/ppermute | solution.py:22
  71.0 2.2 %copy.117 = f32[5,4,128,127]{3,0,2,1:T(8,128)} copy(f32[5,4,128,127]{3,2,1,0:T(8,128)S(1)} %get-tuple-element.15) | data formatting | bytes 2600960
  73.2 2.2 %copy.116 = f32[5,4,128,127]{3,0,2,1:T(8,128)} copy(f32[5,4,128,127]{3,2,1,0:T(8,128)S(1)} %get-tuple-element.16) | data formatting | bytes 2600960
  75.7 1.7 %copy-done.3 = f32[5,6,130,128]{3,0,2,1:T(8,128)} copy-done((f32[5,6,130,128]{3,0,2,1:T(8,128)}, f32[5,6,130,128]{3,0,2,1:T(8,128)S(1)}, u32[]{:S(2)}) %copy-start.3) | copy-done | bytes 1996824
  77.4 3.4 %fusion.20 = f32[4,128,128,5]{2,3,1,0:T(8,128)} fusion(f32[5,6,130,128]{3,0,2,1:T(8,128)S(1)} %maximum_multiply_fusion, f32[1,5,5]{2,0,1:T(1,128)S(1)} %get-tuple-element.18), kind=kOutput, calls=%fused_computation.25 | convolution fusion | flops 19988480 | bytes 5507584 | tf_op jit(solution)/shard_map/fg,gtsa->ftsa/dot_general | solution.py:28
  81.3 1.4 %reduce.1 = f32[32,2560]{1,0:T(8,128)S(1)} reduce(f32[32,1,2560]{2,1,0:T(1,128)S(1)} %all-to-all-done, f32[]{:T(128)} %broadcast.283), dimensions={1}, to_apply=%all_to_all.3.reduce_sub_computation | reduce | bytes 655364 | tf_op jit(solution)/shard_map/all_to_all | solution.py:84
  82.7 0.7 reshape.184
  83.7 0.9 copy.98
  84.5 1.4 %reshape.182 = f32[5,4,128,1]{3,0,2,1:T(8,128)S(1)} reshape(f32[5,4,4,32]{0,3,2,1:T(8,128)} %copy.98) | data formatting | bytes 20480 | tf_op jit(solution)/shard_map/broadcast_in_dim;reshape | solution.py:38
  86.0 4.9 %fusion.18 = f32[4,128,128,5]{2,3,1,0:T(8,128)S(1)} fusion(f32[5,4,128,127]{3,0,2,1:T(8,128)} %copy.116, f32[5,4,128,127]{3,0,2,1:T(8,128)} %copy.117, f32[5,4,128,1]{3,0,2,1:T(8,128)S(1)} %reshape.182, f32[1,5,5]{2,0,1:T(1,128)S(1)} %get-tuple-element.19), kind=kOutput, calls=%fused_computation.23 | convolution fusion | flops 20316160 | bytes 3922020 | tf_op jit(solution)/shard_map/fg,gtsa->ftsa/dot_general | solution.py:28
  90.9 7.1 %fusion.7 = f32[5,4,128,128]{3,0,2,1:T(8,128)S(1)} fusion(f32[4,128,128,5]{2,3,1,0:T(8,128)S(1)} %fusion.18, f32[4,128,128,5]{2,3,1,0:T(8,128)} %fusion.20, f32[5,6,130,128]{3,0,2,1:T(8,128)S(1)} %copy-done.4, f32[5,4,128,127]{3,0,2,1:T(8,128)S(1)} %copy-done.2, f32[4,128,128]{2,1,0:T(8,128)S(1)} %copy-done.5, f32[5,4,128,128]{3,2,1,0:T(8,128)S(1)} %copy-done, ...), kind=kOutput, calls=%fused_computation.14 | convolution fusion | flops 25559040 | bytes 25168384 | tf_op jit(solution)/shard_map/fg,gtsa->ftsa/dot_general | solution.py:28
  98.2 2.0 %collective-permute-start.5 = (f32[5,1,128,128]{3,0,2,1:T(8,128)S(1)}, f32[5,1,128,128]{3,0,2,1:T(8,128)S(1)}, u32[]{:S(2)}, u32[]{:S(2)}) collective-permute-start(f32[5,1,128,128]{3,0,2,1:T(8,128)S(1)} %get-tuple-element.10), channel_id=1, source_target_pairs={{32,0},{64,32},{96,64},{128,96},{160,128},{192,160},{224,192},{0,2... | collective-permute-start | bytes 983048 | tf_op jit(solution)/shard_map/ppermute | solution.py:22
  100.9 7.9 %collective-permute-done.4 = f32[5,1,128,128]{3,0,2,1:T(8,128)S(1)} collective-permute-done((f32[5,1,128,128]{3,0,2,1:T(8,128)S(1)}, f32[5,1,128,128]{3,0,2,1:T(8,128)S(1)}, u32[]{:S(2)}, u32[]{:S(2)}) %collective-permute-start.4) | collective-permute-done | bytes 327712 | tf_op jit(solution)/shard_map/ppermute | solution.py:19
  108.8 2.4 %collective-permute-done.5 = f32[5,1,128,128]{3,0,2,1:T(8,128)S(1)} collective-permute-done((f32[5,1,128,128]{3,0,2,1:T(8,128)S(1)}, f32[5,1,128,128]{3,0,2,1:T(8,128)S(1)}, u32[]{:S(2)}, u32[]{:S(2)}) %collective-permute-start.5) | collective-permute-done | bytes 327712 | tf_op jit(solution)/shard_map/ppermute | solution.py:22
  111.3 5.5 %collective-permute-start.7 = (f32[5,6,1,128]{3,0,2,1:T(8,128)S(1)}, f32[5,6,1,128]{3,0,2,1:T(8,128)S(1)}, u32[]{:S(2)}, u32[]{:S(2)}) collective-permute-start(f32[5,6,1,128]{3,0,2,1:T(8,128)S(1)} %get-tuple-element.6), channel_id=1, source_target_pairs={{1,0},{2,1},{3,2},{4,3},{5,4},{6,5},{7,6},{8,7},{9,8},{10,9},{11,1... | collective-permute-start | bytes 46088 | tf_op jit(solution)/shard_map/ppermute | solution.py:22
  116.8 2.5 %fusion.8 = f32[4,128,128,5]{2,3,1,0:T(8,128)S(1)} fusion(f32[5,4,128,127]{3,0,2,1:T(8,128)S(1)} %get-tuple-element.12, f32[5,4,128,127]{3,0,2,1:T(8,128)S(1)} %get-tuple-element.11, f32[5,4,128,1]{3,0,2,1:T(8,128)S(1)} %reshape.182, f32[1,5,5]{2,0,1:T(1,128)S(1)} %get-tuple-element.19), kind=kOutput, calls=%fused_computation.15 | convolution fusion | flops 20316160 | bytes 3922020 | tf_op jit(solution)/shard_map/fg,gtsa->ftsa/dot_general | solution.py:28
  119.7 2.0 %fusion.10 = f32[4,128,128,5]{2,3,1,0:T(8,128)S(1)} fusion(f32[5,6,130,128]{3,0,2,1:T(8,128)S(1)} %maximum_multiply_fusion.1, f32[1,5,5]{2,0,1:T(1,128)S(1)} %get-tuple-element.18), kind=kOutput, calls=%fused_computation.17 | convolution fusion | flops 19988480 | bytes 5507584 | tf_op jit(solution)/shard_map/fg,gtsa->ftsa/dot_general | solution.py:28
  121.7 5.0 %fusion.3 = f32[5,4,128,128]{3,0,2,1:T(8,128)S(1)} fusion(f32[5,4,128,128]{3,0,2,1:T(8,128)S(1)} %fusion.7, f32[4,128,128,5]{2,3,1,0:T(8,128)S(1)} %fusion.8, f32[4,128,128,5]{2,3,1,0:T(8,128)S(1)} %fusion.10, f32[5,6,130,128]{3,0,2,1:T(8,128)S(1)} %maximum_multiply_fusion.1, f32[5,4,128,127]{3,0,2,1:T(8,128)S(1)} %get-tuple-element.12, ...), kind=kOutput, calls=%fused_computation.9 | convolution fusion | flops 25559040 | bytes 28051968 | tf_op jit(solution)/shard_map/fg,gtsa->ftsa/dot_general | solution.py:28
  126.8 1.3 %copy.90 = f32[5,4,128,128]{3,2,1,0:T(8,128)} copy(f32[5,4,128,128]{3,0,2,1:T(8,128)S(1)} %fusion.3) | data formatting | bytes 2621440 | tf_op jit(solution)/shard_map/sub | solution.py:46
  (59 shorter events, 5.4 us)
Async XLA Ops:
  0.0 5.3 %copy-start.12 = (s32[128]{0:T(128)S(1)}, s32[128]{0:T(128)}, u32[]{:S(2)}) copy-start(s32[128]{0:T(128)} %param.13) | copy-start | bytes 1540
  0.0 5.4 %copy-start.6 = (f32[5,4,128]{2,1,0:T(4,128)S(1)}, f32[5,4,128]{2,1,0:T(4,128)}, u32[]{:S(2)}) copy-start(f32[5,4,128]{2,1,0:T(4,128)} %param.12) | copy-start | bytes 30724
  0.0 5.4 %copy-start.8 = (s32[1,4,4]{2,1,0:T(4,128)S(1)}, s32[1,4,4]{2,1,0:T(4,128)}, u32[]{:S(2)}) copy-start(s32[1,4,4]{2,1,0:T(4,128)} %param.15) | copy-start | bytes 196
  0.0 5.4 %copy-start.9 = (s32[1,4,4]{2,1,0:T(4,128)S(1)}, s32[1,4,4]{2,1,0:T(4,128)}, u32[]{:S(2)}) copy-start(s32[1,4,4]{2,1,0:T(4,128)} %param.14) | copy-start | bytes 196
  0.0 5.5 %copy-start.11 = (f32[16]{0:T(128)S(1)}, f32[16]{0:T(128)}, u32[]{:S(2)}) copy-start(f32[16]{0:T(128)} %param.17) | copy-start | bytes 196
  0.0 5.5 %copy-start.10 = (s32[1,4,4]{2,1,0:T(4,128)S(1)}, s32[1,4,4]{2,1,0:T(4,128)}, u32[]{:S(2)}) copy-start(s32[1,4,4]{2,1,0:T(4,128)} %param.16) | copy-start | bytes 196
  2.2 60.2 %collective-permute-start = (f32[5,1,128,128]{3,0,2,1:T(8,128)}, f32[5,1,128,128]{3,0,2,1:T(8,128)}, u32[]{:S(2)}, u32[]{:S(2)}) collective-permute-start(f32[5,1,128,128]{3,0,2,1:T(8,128)} %copy.118), channel_id=1, source_target_pairs={{0,32},{32,64},{64,96},{96,128},{128,160},{160,192},{192,224},{224... | collective-permute-start | bytes 983048 | tf_op jit(solution)/shard_map/ppermute | solution.py:19
  4.7 59.6 %collective-permute-start.1 = (f32[5,1,128,128]{3,0,2,1:T(8,128)}, f32[5,1,128,128]{3,0,2,1:T(8,128)}, u32[]{:S(2)}, u32[]{:S(2)}) collective-permute-start(f32[5,1,128,128]{3,0,2,1:T(8,128)} %copy.119), channel_id=1, source_target_pairs={{32,0},{64,32},{96,64},{128,96},{160,128},{192,160},{224,192},{0,2... | collective-permute-start | bytes 983048 | tf_op jit(solution)/shard_map/ppermute | solution.py:22
  48.3 13.7 %copy-start.7 = (f32[3,5,5]{2,0,1:T(4,128)S(1)}, f32[3,5,5]{2,0,1:T(4,128)}, u32[]{:S(2)}) copy-start(f32[3,5,5]{2,0,1:T(4,128)} %param.11) | copy-start | bytes 904
  48.3 13.7 %copy-start = (f32[5,4,128,128]{3,2,1,0:T(8,128)S(1)}, f32[5,4,128,128]{3,2,1,0:T(8,128)}, u32[]{:S(2)}) copy-start(f32[5,4,128,128]{3,2,1,0:T(8,128)} %param.9) | copy-start | bytes 3932164
  50.7 30.0 %all-to-all-start = ((f32[32,1,2560]{2,1,0:T(1,128)}), f32[32,1,2560]{2,1,0:T(1,128)S(1)}, u32[]{:S(2)}, u32[]{:S(2)}) async-start(f32[32,1,2560]{2,1,0:T(1,128)} %reshape.183), calls=%async_computation | async-start | bytes 655360 | tf_op jit(solution)/shard_map/all_to_all | solution.py:84
  65.4 9.9 %collective-permute-start.2 = (f32[5,6,1,128]{3,0,2,1:T(8,128)S(1)}, f32[5,6,1,128]{3,0,2,1:T(8,128)S(1)}, u32[]{:S(2)}, u32[]{:S(2)}) collective-permute-start(f32[5,6,1,128]{3,0,2,1:T(8,128)S(1)} %get-tuple-element.7), channel_id=1, source_target_pairs={{0,1},{1,2},{2,3},{3,4},{4,5},{5,6},{6,7},{7,8},{8,9},{9,10},{10,1... | collective-permute-start | bytes 46088 | tf_op jit(solution)/shard_map/ppermute | solution.py:19
  65.8 9.6 %collective-permute-start.3 = (f32[5,6,1,128]{3,0,2,1:T(8,128)S(1)}, f32[5,6,1,128]{3,0,2,1:T(8,128)S(1)}, u32[]{:S(2)}, u32[]{:S(2)}) collective-permute-start(f32[5,6,1,128]{3,0,2,1:T(8,128)S(1)} %get-tuple-element.8), channel_id=1, source_target_pairs={{1,0},{2,1},{3,2},{4,3},{5,4},{6,5},{7,6},{8,7},{9,8},{10,9},{11,1... | collective-permute-start | bytes 46088 | tf_op jit(solution)/shard_map/ppermute | solution.py:22
  75.7 1.7 %copy-start.3 = (f32[5,6,130,128]{3,0,2,1:T(8,128)}, f32[5,6,130,128]{3,0,2,1:T(8,128)S(1)}, u32[]{:S(2)}) copy-start(f32[5,6,130,128]{3,0,2,1:T(8,128)S(1)} %maximum_multiply_fusion) | copy-start | bytes 5990404
  85.9 4.9 %copy-start.1 = (f32[5,4,128,127]{3,0,2,1:T(8,128)S(1)}, f32[5,4,128,127]{3,0,2,1:T(8,128)}, u32[]{:S(2)}) copy-start(f32[5,4,128,127]{3,0,2,1:T(8,128)} %copy.117) | copy-start | bytes 3901444
  86.0 4.9 %copy-start.2 = (f32[5,4,128,127]{3,0,2,1:T(8,128)S(1)}, f32[5,4,128,127]{3,0,2,1:T(8,128)}, u32[]{:S(2)}) copy-start(f32[5,4,128,127]{3,0,2,1:T(8,128)} %copy.116) | copy-start | bytes 3901444
  86.0 4.9 %copy-start.4 = (f32[5,6,130,128]{3,0,2,1:T(8,128)S(1)}, f32[5,6,130,128]{3,0,2,1:T(8,128)}, u32[]{:S(2)}) copy-start(f32[5,6,130,128]{3,0,2,1:T(8,128)} %copy-done.3) | copy-start | bytes 5990404
  86.0 4.9 %copy-start.5 = (f32[4,128,128]{2,1,0:T(8,128)S(1)}, f32[4,128,128]{2,1,0:T(8,128)}, u32[]{:S(2)}) copy-start(f32[4,128,128]{2,1,0:T(8,128)} %param.10) | copy-start | bytes 786436
  98.1 10.7 %collective-permute-start.4 = (f32[5,1,128,128]{3,0,2,1:T(8,128)S(1)}, f32[5,1,128,128]{3,0,2,1:T(8,128)S(1)}, u32[]{:S(2)}, u32[]{:S(2)}) collective-permute-start(f32[5,1,128,128]{3,0,2,1:T(8,128)S(1)} %get-tuple-element.9), channel_id=1, source_target_pairs={{0,32},{32,64},{64,96},{96,128},{128,160},{160,192},{192,224},{224... | collective-permute-start | bytes 983048 | tf_op jit(solution)/shard_map/ppermute | solution.py:19
  98.2 13.1 %collective-permute-start.5 = (f32[5,1,128,128]{3,0,2,1:T(8,128)S(1)}, f32[5,1,128,128]{3,0,2,1:T(8,128)S(1)}, u32[]{:S(2)}, u32[]{:S(2)}) collective-permute-start(f32[5,1,128,128]{3,0,2,1:T(8,128)S(1)} %get-tuple-element.10), channel_id=1, source_target_pairs={{32,0},{64,32},{96,64},{128,96},{160,128},{192,160},{224,192},{0,2... | collective-permute-start | bytes 983048 | tf_op jit(solution)/shard_map/ppermute | solution.py:22
  111.2 8.1 %collective-permute-start.6 = (f32[5,6,1,128]{3,0,2,1:T(8,128)S(1)}, f32[5,6,1,128]{3,0,2,1:T(8,128)S(1)}, u32[]{:S(2)}, u32[]{:S(2)}) collective-permute-start(f32[5,6,1,128]{3,0,2,1:T(8,128)S(1)} %get-tuple-element.5), channel_id=1, source_target_pairs={{0,1},{1,2},{2,3},{3,4},{4,5},{5,6},{6,7},{7,8},{8,9},{9,10},{10,1... | collective-permute-start | bytes 46088 | tf_op jit(solution)/shard_map/ppermute | solution.py:19
  111.3 8.0 %collective-permute-start.7 = (f32[5,6,1,128]{3,0,2,1:T(8,128)S(1)}, f32[5,6,1,128]{3,0,2,1:T(8,128)S(1)}, u32[]{:S(2)}, u32[]{:S(2)}) collective-permute-start(f32[5,6,1,128]{3,0,2,1:T(8,128)S(1)} %get-tuple-element.6), channel_id=1, source_target_pairs={{1,0},{2,1},{3,2},{4,3},{5,4},{6,5},{7,6},{8,7},{9,8},{10,9},{11,1... | collective-permute-start | bytes 46088 | tf_op jit(solution)/shard_map/ppermute | solution.py:22
where the time goes:
time: 128 us
  blocking collectives  36.6 us (29%)
  starting transfers between devices  26.4 us (21%)
  matrix products  26.1 us (20%)
  local copies, waits for them, and re-layouts  25.1 us (20%)
  waiting for transfers between devices  10.4 us (8%)
  other arithmetic  3.01 us (2%)
    all_gather x1, blocking collectives, body(): all_rows = lax.all_gather(rotor_face, 'circ', axis=1, tiled=True)  36.6 us
    dot_general x6, matrix products, contract(): jnp.einsum('fg,gtsa->ftsa', matrix, values, precision=lax.Precision.HIGHEST)  24.9 us
    ppermute x4, starting transfers between devices, with_halo(): lax.ppermute(lax.slice_in_dim(block, 0, width, axis=dim), axis, backward)  13.3 us
    unnamed x35, local copies, waits for them, and re-layouts  12.2 us
    all_to_all x1, starting transfers between devices, body(): received = lax.all_to_all(contributions, 'span', 0, 0, tiled=True)  11.2 us
    ppermute x4, waiting for transfers between devices, with_halo(): lax.ppermute(lax.slice_in_dim(block, block.shape[dim] - width, None, axis...  7.96 us
    gather x1, local copies, waits for them, and re-layouts, body(): rotated = jnp.take_along_axis(all_rows, source_rows[None], axis=1)  3.52 us
  transfers between devices with their start and end apart: 9, of which 2 were waited for; matrix products, arithmetic and copies ran while one was open for 19% of the time, Pallas kernels for 0%

commit v1 on v0

--- a/solution.py
+++ b/solution.py
@@ -65,7 +65,19 @@
     rows_local = rotor_face.shape[1]
     total_rows = rows_local * circ_count
     row_iota = jnp.arange(rows_local, dtype=jnp.int32)
-    all_rows = lax.all_gather(rotor_face, "circ", axis=1, tiled=True)
+
+    def check_leaf_all(d0, local_x):
+        return jnp.concatenate(
+            lax.all_to_all(
+                jnp.stack(lax.axis_size("circ") * [local_x], axis=0),
+                concat_axis=0,
+                split_axis=0,
+                axis_name="circ",
+            ),
+            axis=d0,
+        )
+
+    all_rows = check_leaf_all(1, rotor_face)
     first_row = lax.axis_index("circ") * rows_local
     source_rows = (first_row + row_iota[:, None] - offsets[None, :]) % total_rows
     rotated = jnp.take_along_axis(all_rows, source_rows[None], axis=1)

time: 128 us -> 117 us (0.914)
  blocking collectives: 36.6 us -> 0 us
  waiting for transfers between devices: 10.4 us -> 22.3 us
  local copies, waits for them, and re-layouts: 25.1 us -> 32.8 us
  starting transfers between devices: 26.4 us -> 29.4 us
  other arithmetic: 3.01 us -> 5.79 us
    all_gather x1 -> x0, blocking collectives: 36.6 us -> none  [body(): all_rows = lax.all_gather(rotor_face, 'circ', axis=1, tiled=True)]
    all_to_all x1, waiting for transfers between devices: 0.01 us -> 8.53 us  [body(): received = lax.all_to_all(contributions, 'span', 0, 0, tiled=True)]
    all_to_all x0 -> x1, starting transfers between devices: none -> 5.79 us  [check_leaf_all(): lax.all_to_all(jnp.stack(lax.axis_size('circ') * [local_x], axis=0), conc...]
    all_to_all x1, starting transfers between devices: 11.2 us -> 6.26 us  [body(): received = lax.all_to_all(contributions, 'span', 0, 0, tiled=True)]
    ppermute x4, starting transfers between devices: 2 us -> 4.89 us  [with_halo(): lax.ppermute(lax.slice_in_dim(block, block.shape[dim] - width, None, axis...]
    unnamed x35 -> x34, local copies, waits for them, and re-layouts: 12.2 us -> 15 us
    gather x1, local copies, waits for them, and re-layouts: 3.52 us -> 5.93 us  [body(): rotated = jnp.take_along_axis(all_rows, source_rows[None], axis=1)]
    ppermute x4, waiting for transfers between devices: 2.43 us -> 4.32 us  [with_halo(): lax.ppermute(lax.slice_in_dim(block, 0, width, axis=dim), axis, backward)]
  transfers between devices with their start and end apart: 9 -> 10, of which waited for: 2 -> 3; matrix products, arithmetic and copies ran while one was open for 19% -> 28% of each run, Pallas kernels for 0% -> 0%
where the time goes in v1:
time: 117 us
  local copies, waits for them, and re-layouts  32.8 us (28%)
  starting transfers between devices  29.4 us (25%)
  matrix products  26.1 us (22%)
  waiting for transfers between devices  22.3 us (19%)
  other arithmetic  5.79 us (5%)
    dot_general x6, matrix products, contract(): jnp.einsum('fg,gtsa->ftsa', matrix, values, precision=lax.Precision.HIGHEST)  24.8 us
    unnamed x34, local copies, waits for them, and re-layouts  15 us
    ppermute x4, starting transfers between devices, with_halo(): lax.ppermute(lax.slice_in_dim(block, 0, width, axis=dim), axis, backward)  12.4 us
    ppermute x4, waiting for transfers between devices, with_halo(): lax.ppermute(lax.slice_in_dim(block, block.shape[dim] - width, None, axis...  9.48 us
    all_to_all x1, waiting for transfers between devices, body(): received = lax.all_to_all(contributions, 'span', 0, 0, tiled=True)  8.53 us
    all_to_all x1, starting transfers between devices, body(): received = lax.all_to_all(contributions, 'span', 0, 0, tiled=True)  6.26 us
    gather x1, local copies, waits for them, and re-layouts, body(): rotated = jnp.take_along_axis(all_rows, source_rows[None], axis=1)  5.93 us
    all_to_all x1, starting transfers between devices, check_leaf_all(): lax.all_to_all(jnp.stack(lax.axis_size('circ') * [local_x], axis=0), conc...  5.79 us
  transfers between devices with their start and end apart: 10, of which 3 were waited for; matrix products, arithmetic and copies ran while one was open for 28% of the time, Pallas kernels for 0%

profile of v1, /device:TPU:6, one launch (start us, length us, event | category | flops | bytes accessed | tf_op | source)
XLA Modules:
  0.0 116.8 jit_solution(2070466460169027169)
XLA Ops:
  0.0 1.5 %stack.2 = f32[8,5,4,128]{3,2,1,0:T(4,128)} broadcast(f32[5,4,128]{2,1,0:T(4,128)} %param.12), dimensions={1,2,3} | broadcast | bytes 92160 | tf_op jit(solution)/shard_map/stack | solution.py:72
  1.5 5.8 %all-to-all-start = ((f32[8,5,4,128]{3,2,1,0:T(4,128)}), f32[8,5,4,128]{3,2,1,0:T(4,128)S(1)}, u32[]{:S(2)}, u32[]{:S(2)}) async-start(f32[8,5,4,128]{3,2,1,0:T(4,128)} %stack.2), calls=%async_computation | async-start | bytes 163840 | tf_op jit(solution)/shard_map/all_to_all | solution.py:71
  7.3 1.1 fusion.49
  9.4 1.5 %collective-permute-start = (f32[5,1,128,128]{3,0,2,1:T(8,128)}, f32[5,1,128,128]{3,0,2,1:T(8,128)}, u32[]{:S(2)}, u32[]{:S(2)}) collective-permute-start(f32[5,1,128,128]{3,0,2,1:T(8,128)} %copy.116), channel_id=1, source_target_pairs={{0,32},{32,64},{64,96},{96,128},{128,160},{160,192},{192,224},{224... | collective-permute-start | bytes 983048 | tf_op jit(solution)/shard_map/ppermute | solution.py:19
  12.7 1.5 %fusion.50 = (f32[5,4,128,127]{3,2,1,0:T(8,128)}, f32[5,4,128,127]{3,2,1,0:T(8,128)S(1)}) fusion(f32[5,4,128,128]{3,2,1,0:T(8,128)S(1)} %copy-done), kind=kLoop, calls=%fused_computation.83 | loop fusion | bytes 5201920 | tf_op jit(solution)/shard_map/slice | solution.py:38
  14.7 3.5 %copy.115 = f32[5,4,128,127]{3,0,2,1:T(8,128)} copy(f32[5,4,128,127]{3,2,1,0:T(8,128)} %get-tuple-element.15) | data formatting | bytes 2600960
  18.2 2.2 %copy.114 = f32[5,4,128,127]{3,0,2,1:T(8,128)} copy(f32[5,4,128,127]{3,2,1,0:T(8,128)S(1)} %get-tuple-element.16) | data formatting | bytes 2600960
  21.0 5.9 %gather_fusion = f32[512,5]{1,0:T(8,128)} fusion(f32[5,32,128]{0,2,1:T(8,128)S(1)} %bitcast.67, s32[512]{0:T(512)S(1)} %fusion.41), kind=kCustom, calls=%fused_computation | custom fusion | bytes 24576 | tf_op jit(solution)/shard_map/jit(take_along_axis)/gather | solution.py:83
  26.9 1.1 broadcast_select_fusion
  28.2 1.1 constant_dynamic-update-slice_fusion.1
  30.1 1.1 constant_dynamic-update-slice_fusion
  31.3 1.5 %copy-done.5 = f32[5,6,128,128]{3,0,2,1:T(8,128)} copy-done((f32[5,6,128,128]{3,0,2,1:T(8,128)}, f32[5,6,128,128]{3,0,2,1:T(8,128)S(1)}, u32[]{:S(2)}) %copy-start.5) | copy-done | bytes 1966104
  32.9 6.5 %collective-permute-start.3 = (f32[5,6,1,128]{3,0,2,1:T(8,128)S(1)}, f32[5,6,1,128]{3,0,2,1:T(8,128)S(1)}, u32[]{:S(2)}, u32[]{:S(2)}) collective-permute-start(f32[5,6,1,128]{3,0,2,1:T(8,128)S(1)} %get-tuple-element.8), channel_id=1, source_target_pairs={{1,0},{2,1},{3,2},{4,3},{5,4},{6,5},{7,6},{8,7},{9,8},{10,9},{11,1... | collective-permute-start | bytes 46088 | tf_op jit(solution)/shard_map/ppermute | solution.py:22
  39.4 1.2 %fusion.34 = f32[32,4,5,4,32]{4,0,3,2,1:T(8,128)S(1)} fusion(f32[32,4,4,1,1]{0,2,4,3,1:T(4,128)S(1)} %copy.91, f32[5,4,4,32]{3,2,1,0:T(4,128)S(1)} %copy.95), kind=kOutput, calls=%fused_computation.39 | convolution fusion | flops 3932160 | bytes 339968 | tf_op jit(solution)/shard_map/gk,ftkp->gftp/dot_general | solution.py:94
  41.5 1.6 %reshape.193 = f32[32,1,2560]{2,1,0:T(1,128)} reshape(f32[32,4,5,4,32]{4,3,2,1,0:T(4,128)S(1)} %copy.78) | data formatting | bytes 655360
  43.1 6.3 %all-to-all-start.1 = ((f32[32,1,2560]{2,1,0:T(1,128)}), f32[32,1,2560]{2,1,0:T(1,128)S(1)}, u32[]{:S(2)}, u32[]{:S(2)}) async-start(f32[32,1,2560]{2,1,0:T(1,128)} %reshape.193), calls=%async_computation.1 | async-start | bytes 655360 | tf_op jit(solution)/shard_map/all_to_all | solution.py:96
  49.3 2.2 %maximum_multiply_fusion = f32[5,6,130,128]{3,0,2,1:T(8,128)S(1)} fusion(f32[5,6,1,128]{3,0,2,1:T(8,128)S(1)} %collective-permute-done.3, f32[5,6,128,128]{3,0,2,1:T(8,128)} %copy-done.5, f32[5,6,1,128]{3,0,2,1:T(8,128)S(1)} %collective-permute-done.2, f32[130]{0:T(256)S(1)} %not_convert_fusion), kind=kLoop, calls=%fused_computation.1 | loop fusion | flops 1497600 | bytes 3994120 | tf_op jit(solution)/shard_map/mul | solution.py:58
  51.6 1.6 %copy-done.3 = f32[5,6,130,128]{3,0,2,1:T(8,128)} copy-done((f32[5,6,130,128]{3,0,2,1:T(8,128)}, f32[5,6,130,128]{3,0,2,1:T(8,128)S(1)}, u32[]{:S(2)}) %copy-start.3) | copy-done | bytes 1996824
  53.2 3.4 %fusion.20 = f32[4,128,128,5]{2,3,1,0:T(8,128)} fusion(f32[5,6,130,128]{3,0,2,1:T(8,128)S(1)} %maximum_multiply_fusion, f32[1,5,5]{2,0,1:T(1,128)S(1)} %get-tuple-element.18), kind=kOutput, calls=%fused_computation.25 | convolution fusion | flops 19988480 | bytes 5507584 | tf_op jit(solution)/shard_map/fg,gtsa->ftsa/dot_general | solution.py:28
  56.6 8.5 %all-to-all-done.1 = f32[32,1,2560]{2,1,0:T(1,128)S(1)} async-done(((f32[32,1,2560]{2,1,0:T(1,128)}), f32[32,1,2560]{2,1,0:T(1,128)S(1)}, u32[]{:S(2)}, u32[]{:S(2)}) %all-to-all-start.1) | async-done | bytes 327712 | tf_op jit(solution)/shard_map/all_to_all | solution.py:96
  65.6 1.4 %reduce.1 = f32[32,2560]{1,0:T(8,128)S(1)} reduce(f32[32,1,2560]{2,1,0:T(1,128)S(1)} %all-to-all-done.1, f32[]{:T(128)} %broadcast.285), dimensions={1}, to_apply=%all_to_all.7.reduce_sub_computation | reduce | bytes 655364 | tf_op jit(solution)/shard_map/all_to_all | solution.py:96
  68.9 1.4 %reshape.192 = f32[5,4,128,1]{3,0,2,1:T(8,128)S(1)} reshape(f32[5,4,4,32]{0,3,2,1:T(8,128)} %copy.96) | data formatting | bytes 20480 | tf_op jit(solution)/shard_map/broadcast_in_dim;reshape | solution.py:38
  70.4 4.9 %fusion.18 = f32[4,128,128,5]{2,3,1,0:T(8,128)S(1)} fusion(f32[5,4,128,127]{3,0,2,1:T(8,128)} %copy.114, f32[5,4,128,127]{3,0,2,1:T(8,128)} %copy.115, f32[5,4,128,1]{3,0,2,1:T(8,128)S(1)} %reshape.192, f32[1,5,5]{2,0,1:T(1,128)S(1)} %get-tuple-element.19), kind=kOutput, calls=%fused_computation.23 | convolution fusion | flops 20316160 | bytes 3922020 | tf_op jit(solution)/shard_map/fg,gtsa->ftsa/dot_general | solution.py:28
  75.3 7.1 %fusion.7 = f32[5,4,128,128]{3,0,2,1:T(8,128)S(1)} fusion(f32[4,128,128,5]{2,3,1,0:T(8,128)S(1)} %fusion.18, f32[4,128,128,5]{2,3,1,0:T(8,128)} %fusion.20, f32[5,6,130,128]{3,0,2,1:T(8,128)S(1)} %copy-done.4, f32[5,4,128,127]{3,0,2,1:T(8,128)S(1)} %copy-done.2, f32[4,128,128]{2,1,0:T(8,128)S(1)} %copy-done.6, f32[5,4,128,128]{3,2,1,0:T(8,128)S(1)} %copy-done, ...), kind=kOutput, calls=%fused_computation.14 | convolution fusion | flops 25559040 | bytes 25168384 | tf_op jit(solution)/shard_map/fg,gtsa->ftsa/dot_general | solution.py:28
  82.4 3.0 %collective-permute-start.4 = (f32[5,1,128,128]{3,0,2,1:T(8,128)S(1)}, f32[5,1,128,128]{3,0,2,1:T(8,128)S(1)}, u32[]{:S(2)}, u32[]{:S(2)}) collective-permute-start(f32[5,1,128,128]{3,0,2,1:T(8,128)S(1)} %get-tuple-element.9), channel_id=1, source_target_pairs={{0,32},{32,64},{64,96},{96,128},{128,160},{160,192},{192,224},{224... | collective-permute-start | bytes 983048 | tf_op jit(solution)/shard_map/ppermute | solution.py:19
  86.2 9.5 %collective-permute-done.4 = f32[5,1,128,128]{3,0,2,1:T(8,128)S(1)} collective-permute-done((f32[5,1,128,128]{3,0,2,1:T(8,128)S(1)}, f32[5,1,128,128]{3,0,2,1:T(8,128)S(1)}, u32[]{:S(2)}, u32[]{:S(2)}) %collective-permute-start.4) | collective-permute-done | bytes 327712 | tf_op jit(solution)/shard_map/ppermute | solution.py:19
  95.6 4.3 %collective-permute-done.5 = f32[5,1,128,128]{3,0,2,1:T(8,128)S(1)} collective-permute-done((f32[5,1,128,128]{3,0,2,1:T(8,128)S(1)}, f32[5,1,128,128]{3,0,2,1:T(8,128)S(1)}, u32[]{:S(2)}, u32[]{:S(2)}) %collective-permute-start.5) | collective-permute-done | bytes 327712 | tf_op jit(solution)/shard_map/ppermute | solution.py:22
  100.3 5.3 %collective-permute-start.7 = (f32[5,6,1,128]{3,0,2,1:T(8,128)S(1)}, f32[5,6,1,128]{3,0,2,1:T(8,128)S(1)}, u32[]{:S(2)}, u32[]{:S(2)}) collective-permute-start(f32[5,6,1,128]{3,0,2,1:T(8,128)S(1)} %get-tuple-element.6), channel_id=1, source_target_pairs={{1,0},{2,1},{3,2},{4,3},{5,4},{6,5},{7,6},{8,7},{9,8},{10,9},{11,1... | collective-permute-start | bytes 46088 | tf_op jit(solution)/shard_map/ppermute | solution.py:22
  105.6 2.5 %fusion.8 = f32[4,128,128,5]{2,3,1,0:T(8,128)S(1)} fusion(f32[5,4,128,127]{3,0,2,1:T(8,128)S(1)} %get-tuple-element.12, f32[5,4,128,127]{3,0,2,1:T(8,128)S(1)} %get-tuple-element.11, f32[5,4,128,1]{3,0,2,1:T(8,128)S(1)} %reshape.192, f32[1,5,5]{2,0,1:T(1,128)S(1)} %get-tuple-element.19), kind=kOutput, calls=%fused_computation.15 | convolution fusion | flops 20316160 | bytes 3922020 | tf_op jit(solution)/shard_map/fg,gtsa->ftsa/dot_general | solution.py:28
  108.5 2.0 %fusion.10 = f32[4,128,128,5]{2,3,1,0:T(8,128)S(1)} fusion(f32[5,6,130,128]{3,0,2,1:T(8,128)S(1)} %maximum_multiply_fusion.1, f32[1,5,5]{2,0,1:T(1,128)S(1)} %get-tuple-element.18), kind=kOutput, calls=%fused_computation.17 | convolution fusion | flops 19988480 | bytes 5507584 | tf_op jit(solution)/shard_map/fg,gtsa->ftsa/dot_general | solution.py:28
  110.5 5.0 %fusion.3 = f32[5,4,128,128]{3,0,2,1:T(8,128)S(1)} fusion(f32[5,4,128,128]{3,0,2,1:T(8,128)S(1)} %fusion.7, f32[4,128,128,5]{2,3,1,0:T(8,128)S(1)} %fusion.8, f32[4,128,128,5]{2,3,1,0:T(8,128)S(1)} %fusion.10, f32[5,6,130,128]{3,0,2,1:T(8,128)S(1)} %maximum_multiply_fusion.1, f32[5,4,128,127]{3,0,2,1:T(8,128)S(1)} %get-tuple-element.12, ...), kind=kOutput, calls=%fused_computation.9 | convolution fusion | flops 25559040 | bytes 28051968 | tf_op jit(solution)/shard_map/fg,gtsa->ftsa/dot_general | solution.py:28
  115.5 1.3 %copy.88 = f32[5,4,128,128]{3,2,1,0:T(8,128)} copy(f32[5,4,128,128]{3,0,2,1:T(8,128)S(1)} %fusion.3) | data formatting | bytes 2621440 | tf_op jit(solution)/shard_map/sub | solution.py:46
  (60 shorter events, 9.6 us)
Async XLA Ops:
  0.0 12.6 %copy-start = (f32[5,4,128,128]{3,2,1,0:T(8,128)S(1)}, f32[5,4,128,128]{3,2,1,0:T(8,128)}, u32[]{:S(2)}) copy-start(f32[5,4,128,128]{3,2,1,0:T(8,128)} %param.9) | copy-start | bytes 3932164
  0.0 12.4 %copy-start.12 = (s32[128]{0:T(128)S(1)}, s32[128]{0:T(128)}, u32[]{:S(2)}) copy-start(s32[128]{0:T(128)} %param.13) | copy-start | bytes 1540
  1.5 18.9 %all-to-all-start = ((f32[8,5,4,128]{3,2,1,0:T(4,128)}), f32[8,5,4,128]{3,2,1,0:T(4,128)S(1)}, u32[]{:S(2)}, u32[]{:S(2)}) async-start(f32[8,5,4,128]{3,2,1,0:T(4,128)} %stack.2), calls=%async_computation | async-start | bytes 163840 | tf_op jit(solution)/shard_map/all_to_all | solution.py:71
  9.4 18.8 %collective-permute-start = (f32[5,1,128,128]{3,0,2,1:T(8,128)}, f32[5,1,128,128]{3,0,2,1:T(8,128)}, u32[]{:S(2)}, u32[]{:S(2)}) collective-permute-start(f32[5,1,128,128]{3,0,2,1:T(8,128)} %copy.116), channel_id=1, source_target_pairs={{0,32},{32,64},{64,96},{96,128},{128,160},{160,192},{192,224},{224... | collective-permute-start | bytes 983048 | tf_op jit(solution)/shard_map/ppermute | solution.py:19
  11.9 18.3 %collective-permute-start.1 = (f32[5,1,128,128]{3,0,2,1:T(8,128)}, f32[5,1,128,128]{3,0,2,1:T(8,128)}, u32[]{:S(2)}, u32[]{:S(2)}) collective-permute-start(f32[5,1,128,128]{3,0,2,1:T(8,128)} %copy.117), channel_id=1, source_target_pairs={{32,0},{64,32},{96,64},{128,96},{160,128},{192,160},{224,192},{0,2... | collective-permute-start | bytes 983048 | tf_op jit(solution)/shard_map/ppermute | solution.py:22
  12.6 1.6 %copy-start.7 = (f32[3,5,5]{2,0,1:T(4,128)S(1)}, f32[3,5,5]{2,0,1:T(4,128)}, u32[]{:S(2)}) copy-start(f32[3,5,5]{2,0,1:T(4,128)} %param.11) | copy-start | bytes 904
  12.6 1.6 %copy-start.8 = (s32[1,4,4]{2,1,0:T(4,128)S(1)}, s32[1,4,4]{2,1,0:T(4,128)}, u32[]{:S(2)}) copy-start(s32[1,4,4]{2,1,0:T(4,128)} %param.15) | copy-start | bytes 196
  12.6 1.6 %copy-start.9 = (s32[1,4,4]{2,1,0:T(4,128)S(1)}, s32[1,4,4]{2,1,0:T(4,128)}, u32[]{:S(2)}) copy-start(s32[1,4,4]{2,1,0:T(4,128)} %param.14) | copy-start | bytes 196
  12.6 1.6 %copy-start.10 = (s32[1,4,4]{2,1,0:T(4,128)S(1)}, s32[1,4,4]{2,1,0:T(4,128)}, u32[]{:S(2)}) copy-start(s32[1,4,4]{2,1,0:T(4,128)} %param.16) | copy-start | bytes 196
  12.7 1.6 %copy-start.11 = (f32[16]{0:T(128)S(1)}, f32[16]{0:T(128)}, u32[]{:S(2)}) copy-start(f32[16]{0:T(128)} %param.17) | copy-start | bytes 196
  31.2 1.7 %copy-start.5 = (f32[5,6,128,128]{3,0,2,1:T(8,128)}, f32[5,6,128,128]{3,0,2,1:T(8,128)S(1)}, u32[]{:S(2)}) copy-start(f32[5,6,128,128]{3,0,2,1:T(8,128)S(1)} %constant_dynamic-update-slice_fusion) | copy-start | bytes 5898244
  31.2 18.1 %collective-permute-start.2 = (f32[5,6,1,128]{3,0,2,1:T(8,128)S(1)}, f32[5,6,1,128]{3,0,2,1:T(8,128)S(1)}, u32[]{:S(2)}, u32[]{:S(2)}) collective-permute-start(f32[5,6,1,128]{3,0,2,1:T(8,128)S(1)} %get-tuple-element.7), channel_id=1, source_target_pairs={{0,1},{1,2},{2,3},{3,4},{4,5},{5,6},{6,7},{7,8},{8,9},{9,10},{10,1... | collective-permute-start | bytes 46088 | tf_op jit(solution)/shard_map/ppermute | solution.py:19
  32.9 16.5 %collective-permute-start.3 = (f32[5,6,1,128]{3,0,2,1:T(8,128)S(1)}, f32[5,6,1,128]{3,0,2,1:T(8,128)S(1)}, u32[]{:S(2)}, u32[]{:S(2)}) collective-permute-start(f32[5,6,1,128]{3,0,2,1:T(8,128)S(1)} %get-tuple-element.8), channel_id=1, source_target_pairs={{1,0},{2,1},{3,2},{4,3},{5,4},{6,5},{7,6},{8,7},{9,8},{10,9},{11,1... | collective-permute-start | bytes 46088 | tf_op jit(solution)/shard_map/ppermute | solution.py:22
  43.1 22.1 %all-to-all-start.1 = ((f32[32,1,2560]{2,1,0:T(1,128)}), f32[32,1,2560]{2,1,0:T(1,128)S(1)}, u32[]{:S(2)}, u32[]{:S(2)}) async-start(f32[32,1,2560]{2,1,0:T(1,128)} %reshape.193), calls=%async_computation.1 | async-start | bytes 655360 | tf_op jit(solution)/shard_map/all_to_all | solution.py:96
  51.6 1.7 %copy-start.3 = (f32[5,6,130,128]{3,0,2,1:T(8,128)}, f32[5,6,130,128]{3,0,2,1:T(8,128)S(1)}, u32[]{:S(2)}) copy-start(f32[5,6,130,128]{3,0,2,1:T(8,128)S(1)} %maximum_multiply_fusion) | copy-start | bytes 5990404
  70.3 4.9 %copy-start.1 = (f32[5,4,128,127]{3,0,2,1:T(8,128)S(1)}, f32[5,4,128,127]{3,0,2,1:T(8,128)}, u32[]{:S(2)}) copy-start(f32[5,4,128,127]{3,0,2,1:T(8,128)} %copy.115) | copy-start | bytes 3901444
  70.3 4.9 %copy-start.2 = (f32[5,4,128,127]{3,0,2,1:T(8,128)S(1)}, f32[5,4,128,127]{3,0,2,1:T(8,128)}, u32[]{:S(2)}) copy-start(f32[5,4,128,127]{3,0,2,1:T(8,128)} %copy.114) | copy-start | bytes 3901444
  70.3 4.9 %copy-start.4 = (f32[5,6,130,128]{3,0,2,1:T(8,128)S(1)}, f32[5,6,130,128]{3,0,2,1:T(8,128)}, u32[]{:S(2)}) copy-start(f32[5,6,130,128]{3,0,2,1:T(8,128)} %copy-done.3) | copy-start | bytes 5990404
  70.3 4.9 %copy-start.6 = (f32[4,128,128]{2,1,0:T(8,128)S(1)}, f32[4,128,128]{2,1,0:T(8,128)}, u32[]{:S(2)}) copy-start(f32[4,128,128]{2,1,0:T(8,128)} %param.10) | copy-start | bytes 786436
  82.4 13.2 %collective-permute-start.4 = (f32[5,1,128,128]{3,0,2,1:T(8,128)S(1)}, f32[5,1,128,128]{3,0,2,1:T(8,128)S(1)}, u32[]{:S(2)}, u32[]{:S(2)}) collective-permute-start(f32[5,1,128,128]{3,0,2,1:T(8,128)S(1)} %get-tuple-element.9), channel_id=1, source_target_pairs={{0,32},{32,64},{64,96},{96,128},{128,160},{160,192},{192,224},{224... | collective-permute-start | bytes 983048 | tf_op jit(solution)/shard_map/ppermute | solution.py:19
  85.5 14.5 %collective-permute-start.5 = (f32[5,1,128,128]{3,0,2,1:T(8,128)S(1)}, f32[5,1,128,128]{3,0,2,1:T(8,128)S(1)}, u32[]{:S(2)}, u32[]{:S(2)}) collective-permute-start(f32[5,1,128,128]{3,0,2,1:T(8,128)S(1)} %get-tuple-element.10), channel_id=1, source_target_pairs={{32,0},{64,32},{96,64},{128,96},{160,128},{192,160},{224,192},{0,2... | collective-permute-start | bytes 983048 | tf_op jit(solution)/shard_map/ppermute | solution.py:22
  100.0 8.1 %collective-permute-start.6 = (f32[5,6,1,128]{3,0,2,1:T(8,128)S(1)}, f32[5,6,1,128]{3,0,2,1:T(8,128)S(1)}, u32[]{:S(2)}, u32[]{:S(2)}) collective-permute-start(f32[5,6,1,128]{3,0,2,1:T(8,128)S(1)} %get-tuple-element.5), channel_id=1, source_target_pairs={{0,1},{1,2},{2,3},{3,4},{4,5},{5,6},{6,7},{7,8},{8,9},{9,10},{10,1... | collective-permute-start | bytes 46088 | tf_op jit(solution)/shard_map/ppermute | solution.py:19
  100.3 7.8 %collective-permute-start.7 = (f32[5,6,1,128]{3,0,2,1:T(8,128)S(1)}, f32[5,6,1,128]{3,0,2,1:T(8,128)S(1)}, u32[]{:S(2)}, u32[]{:S(2)}) collective-permute-start(f32[5,6,1,128]{3,0,2,1:T(8,128)S(1)} %get-tuple-element.6), channel_id=1, source_target_pairs={{1,0},{2,1},{3,2},{4,3},{5,4},{6,5},{7,6},{8,7},{9,8},{10,9},{11,1... | collective-permute-start | bytes 46088 | tf_op jit(solution)/shard_map/ppermute | solution.py:22
